TPU v7x, 32 devices: a whole 2x2x4 slice. The times are simulated.
32 devices in a mesh: uv: 8 (over y, x, core), chan: 4 (over z).
Axes of the slice: x: 2, y: 2, z: 4, core: 2. Of those that a mesh axis runs over, the one named last changes fastest.
Arguments:
- vis: bfloat16 [98304, 2, 1024], P('uv', None, 'chan'), may hold values from -6 to 6
- row_cell: int32 [98304], P('uv'), may hold values from 0 to 127
- tap_weight: bfloat16 [8, 98304], P(None, 'uv'), may hold values from 0.029907227 to 0.29882812
- tap_offset: int32 [8], replicated, may hold values from -32 to 32
- block_tile: int32 [768], P('uv'), may hold values from 0 to 79, as said below
- tile_owner: int32 [80], replicated, may hold values from 0 to 7, as said below
- galaxy: bfloat16 [152, 128, 2048], P('uv', 'chan'), may hold values from -6 to 6
Outputs:
- delay_cube: bfloat16 [152, 128, 2048], P('uv', 'chan')
- cross_power: float32 [152, 1024], P('uv')
Inputs may be any that keep to these rules, and one draw needn't show every extreme that they name: `tile_owner`: each of the 8 owners holds 1 to 19 tiles, and some owner exactly 19. `block_tile`: of the 96 row blocks of one index of uv, at most 22 lie in tiles of one owner, and exactly 22 lie in the tiles of some owner.
All inputs are finite; a program needn't handle non-finite values.
Results may differ from a plain program's by a relative error of at most 0.0059.
Values may be sent and summed in bfloat16 or wider, within the bound.
No kernel may reach another device: no remote copies, remote signals or barrier semaphores. Data moves between devices by JAX's collectives and lax.ppermute only.
A program may use at most 128 MiB of HBM per device.

v0:
```python
import math
import jax
import jax.numpy as jnp
from jax import lax
from jax.sharding import PartitionSpec as P

CH = 1024
BR = 128
TC = 128
KT = 8


def tile_ranks(tile_owner, owners):
    onehot = (tile_owner[:, None] == jnp.arange(owners, dtype=jnp.int32)[None, :]).astype(jnp.int32)
    before = jnp.cumsum(onehot, axis=0) - onehot
    return jnp.sum(before * onehot, axis=1)


def kernel_matrix(cells, weights, tap_offset):
    positions = jnp.arange(TC, dtype=jnp.int32)
    total = jnp.zeros(cells.shape[:-1] + (TC, cells.shape[-1]), jnp.float32)
    for k in range(KT):
        target = cells + tap_offset[k]
        hit = target[..., None, :] == positions[:, None]
        total = total + jnp.where(
            hit, weights[..., k, :].astype(jnp.float32)[..., None, :], jnp.float32(0.0)
        )
    return total.astype(jnp.bfloat16)


def delay_table():
    freq = jnp.arange(CH, dtype=jnp.int32)
    phase = (freq[:, None] * freq[None, :] % CH).astype(jnp.float32) * jnp.float32(
        2.0 * math.pi / CH
    )
    cosine = jnp.cos(phase)
    sine = jnp.sin(phase)
    x = freq.astype(jnp.float32) * jnp.float32(2.0 * math.pi / CH)
    taper = 0.35875 - 0.48829 * jnp.cos(x) + 0.14128 * jnp.cos(2.0 * x) - 0.01168 * jnp.cos(3.0 * x)
    scale = (taper / jnp.float32(math.sqrt(CH)))[:, None]
    upper = jnp.concatenate([cosine * scale, -sine * scale], axis=1)
    lower = jnp.concatenate([sine * scale, cosine * scale], axis=1)
    return jnp.concatenate([upper, lower], axis=0).astype(jnp.bfloat16)


def _partner_pairs(n, fn):
    return [(i, fn(i)) for i in range(n)]


def _allreduce_sum(x, axis, n):
    if n & n - 1:
        return lax.psum(x, axis)
    d = 1
    while d < n:
        x = x + lax.ppermute(x, axis, _partner_pairs(n, lambda i, d=d: i ^ d))
        d *= 2
    return x


def _gather_pair(part, matrix, pick2, parity, chip, n_owners, slots_dev, after=None):
    pairs = n_owners // 2
    contrib = jnp.einsum("bcr,brf->bcf", matrix, part, preferred_element_type=jnp.float32)
    high = contrib.astype(jnp.bfloat16)
    low = (contrib - high.astype(jnp.float32)).astype(jnp.bfloat16)
    partial = jnp.einsum(
        "sb,bcf->scf",
        pick2,
        jnp.concatenate([high, low], axis=0),
        preferred_element_type=jnp.float32,
    ).astype(jnp.bfloat16)
    partial = partial.reshape((2, pairs, slots_dev) + partial.shape[1:])
    mine = lax.dynamic_index_in_dim(partial, parity, axis=0, keepdims=False)
    other = lax.dynamic_index_in_dim(partial, 1 - parity, axis=0, keepdims=False)
    if after is not None:
        other, _ = lax.optimization_barrier((other, after))
    got = lax.ppermute(other, "uv", _partner_pairs(n_owners, lambda i: i ^ 1))
    pair_send = (mine.astype(jnp.float32) + got.astype(jnp.float32)).astype(jnp.bfloat16)
    own = lax.dynamic_index_in_dim(mine, chip, axis=0, keepdims=False).astype(
        jnp.float32
    ) + lax.dynamic_index_in_dim(got, chip, axis=0, keepdims=False).astype(jnp.float32)
    return (pair_send, own)


def _scatter_pairs(pair_send, own, chip, n_owners):
    pairs = n_owners // 2
    grid = own
    for d in range(1, pairs):
        if pairs & pairs - 1:
            dest = lambda c, d=d: (c + d) % pairs
        else:
            dest = lambda c, d=d: c ^ d
        send = lax.dynamic_index_in_dim(pair_send, dest(chip), axis=0, keepdims=False)
        recv = lax.ppermute(
            send, "uv", _partner_pairs(n_owners, lambda i, dest=dest: dest(i // 2) * 2 + i % 2)
        )
        grid = grid + recv.astype(jnp.float32)
    return grid.astype(jnp.bfloat16)


def body(vis, row_cell, tap_weight, tap_offset, block_tile, tile_owner, galaxy):
    n_owners = lax.axis_size("uv")
    n_chan = lax.axis_size("chan")
    pairs = n_owners // 2
    me = lax.axis_index("uv")
    parity = me % 2
    chip = me // 2
    nblocks = block_tile.shape[0]
    slots_dev = galaxy.shape[0]
    chan_dev = vis.shape[2]
    rank_of_tile = tile_ranks(tile_owner, n_owners)
    owner = tile_owner[block_tile]
    rank = rank_of_tile[block_tile]
    slot = owner % 2 * (pairs * slots_dev) + owner // 2 * slots_dev + rank
    n_slots = n_owners * slots_dev
    pick = (jnp.arange(n_slots, dtype=jnp.int32)[:, None] == slot[None, :]).astype(jnp.bfloat16)
    pick2 = jnp.concatenate([pick, pick], axis=1)
    width = 2 * chan_dev
    blocks = vis.reshape(nblocks, BR, width)
    cells = row_cell.reshape(nblocks, BR)
    weights = jnp.transpose(tap_weight.reshape(KT, nblocks, BR), (1, 0, 2))
    matrix = kernel_matrix(cells, weights, tap_offset)
    table = delay_table()
    cut = width - width // 4
    first = _gather_pair(blocks[:, :, :cut], matrix, pick2, parity, chip, n_owners, slots_dev)
    first_grid = _scatter_pairs(first[0], first[1], chip, n_owners)
    second = _gather_pair(
        blocks[:, :, cut:], matrix, pick2, parity, chip, n_owners, slots_dev, after=first_grid
    )
    table, first_grid = lax.optimization_barrier((table, first_grid))
    second_grid = _scatter_pairs(second[0], second[1], chip, n_owners)
    by_source = table.reshape(2, n_chan, chan_dev, 2 * CH).transpose(1, 0, 2, 3)
    by_source = by_source.reshape(n_chan, width, 2 * CH)
    out = None
    for gridded, lo, hi in ((first_grid, 0, cut), (second_grid, cut, width)):
        piece = lax.all_to_all(gridded, "chan", split_axis=1, concat_axis=2, tiled=True)
        count, cells_part = (piece.shape[0], piece.shape[1])
        rows = by_source[:, lo:hi, :].reshape(n_chan * (hi - lo), 2 * CH)
        term = jnp.dot(
            piece.reshape(count * cells_part, n_chan * (hi - lo)),
            rows,
            preferred_element_type=jnp.float32,
        )
        out = term if out is None else out + term
    delay = out.reshape(count, cells_part, 2 * CH)
    galaxy_f = galaxy.astype(jnp.float32)
    product = delay[..., :CH] * galaxy_f[..., :CH] + delay[..., CH:] * galaxy_f[..., CH:]
    local_power = jnp.sum(product, axis=1)
    power = _allreduce_sum(local_power, "chan", n_chan) / jnp.float32(math.sqrt(TC))
    return (delay.astype(jnp.bfloat16), power)


def solution(mesh):
    return jax.shard_map(
        body,
        mesh=mesh,
        in_specs=(
            P("uv", None, "chan"),
            P("uv"),
            P(None, "uv"),
            P(),
            P("uv"),
            P(),
            P("uv", "chan", None),
        ),
        out_specs=(P("uv", "chan", None), P("uv", None)),
        check_vma=False,
    )
```

profile of v0, /device:TPU:0, one launch (start us, length us, event | category | flops | bytes accessed | tf_op | source)
XLA Modules:
  0.0 397.5 jit_solution(489984688012996538)
XLA Ops:
  0.6 1.6 fusion.41
  2.3 2.4 slice_convert_fusion.7
  4.7 0.0 copy-start.23
  4.7 0.0 copy-start
  4.7 0.0 copy-start.4
  4.7 20.5 %reshape.165 = bf16[96,128,512]{2,1,0:T(8,128)(2,1)} reshape(bf16[12288,2,256]{2,1,0:T(2,128)(2,1)} %param.7) | data formatting | bytes 25165824 | tf_op jit(solution)/shard_map/reshape | solution.py:118
  25.3 0.1 fusion.35
  25.3 0.1 reduce_window_sum.11
  25.5 0.2 select_reduce_fusion
  25.6 1.2 gather_fusion
  26.9 1.2 gather_fusion.1
  28.2 5.0 %add_bitcast_fusion.10 = (s32[96,128]{1,0:T(8,128)S(1)}, s32[96,128]{1,0:T(8,128)S(1)}, s32[96,128]{1,0:T(8,128)S(1)}, s32[96,128]{1,0:T(8,128)S(1)}, s32[96,128...) fusion(s32[12288]{0:T(1024)S(1)} %copy-done.4, s32[]{:T(128)} %bitcast.1, ...), kind=kLoop, calls=%fused_computation.86 | loop fusion | flops 98304 | bytes 442400 | tf_op jit(solution)/shard_map/add | solution.py:23
  33.3 14.2 %subtract_convert_fusion = (bf16[96,128,384]{2,1,0:T(8,128)(2,1)}, bf16[96,128,384]{2,1,0:T(8,128)(2,1)}) fusion(bf16[96,128,512]{2,1,0:T(8,128)(2,1)} %reshape.165, f32[96,128]{1,0:T(8,128)S(1)} %bitcast.120, s32[96,128]{1,0:T(8,128)S(1)} %get-tuple-element.32, f32[96,128]{1,0:T(8,128)S(1)} %bitcast.122, s32[96,128]{1,0:T(8,128)S(1)} %get-tuple-element.33, ...), kind=kOutput, calls=%fused_computation.5 | convolution fusion | flops 1264582656 | bytes 29097984 | tf_op jit(solution)/shard_map/bcr,brf->bcf/dot_general | solution.py:62
  47.5 15.3 %pad_maximum_fusion = bf16[192,128,384]{2,1,0:T(8,128)(2,1)} fusion(bf16[96,128,384]{2,1,0:T(8,128)(2,1)} %get-tuple-element.10, bf16[96,128,384]{2,1,0:T(8,128)(2,1)} %get-tuple-element.11), kind=kLoop, calls=%fused_computation.2 | loop fusion | flops 9437184 | bytes 37748736 | tf_op jit(solution)/shard_map/concatenate | solution.py:68
  62.8 30.0 %fusion.3 = bf16[152,128,384]{2,0,1:T(8,128)(2,1)} fusion(bf16[192,128,384]{2,1,0:T(8,128)(2,1)} %pad_maximum_fusion, pred[152,96]{1,0:T(8,128)(4,1)S(1)} %iota_compare_fusion.8), kind=kOutput, calls=%fused_computation.8 | convolution fusion | flops 2876404224 | bytes 33831168 | tf_op jit(solution)/shard_map/sb,bcf->scf/dot_general | solution.py:65
  92.8 11.9 %copy.27 = bf16[152,128,384]{2,1,0:T(8,128)(2,1)} copy(bf16[152,128,384]{2,0,1:T(8,128)(2,1)} %fusion.3) | data formatting | bytes 29884416 | tf_op jit(solution)/shard_map/convert_element_type | solution.py:70
  104.6 7.6 %dynamic-slice_bitcast_fusion = bf16[4,19,128,384]{3,2,1,0:T(8,128)(2,1)} fusion(bf16[2,4,19,128,384]{4,3,2,1,0:T(8,128)(2,1)} %bitcast.97, s32[]{:T(128)S(6)} %select_n.123), kind=kLoop, calls=%fused_computation.12 | loop fusion | bytes 14942212 | tf_op jit(solution)/shard_map/jit(dynamic_index_in_dim)/squeeze | solution.py:73
  112.2 0.5 collective-permute-start
  112.7 11.8 %collective-permute-done = bf16[4,19,128,384]{3,2,1,0:T(8,128)(2,1)} collective-permute-done((bf16[4,19,128,384]{3,2,1,0:T(8,128)(2,1)}, bf16[4,19,128,384]{3,2,1,0:T(8,128)(2,1)}, u32[]{:S(2)}, u32[]{:S(2)}) %collective-permute-start) | collective-permute-done | bytes 7471136 | tf_op jit(solution)/shard_map/ppermute | solution.py:76
  124.5 11.9 %fusion.2 = bf16[4,19,128,384]{3,2,1,0:T(8,128)(2,1)} fusion(bf16[4,19,128,384]{3,2,1,0:T(8,128)(2,1)} %collective-permute-done, bf16[2,4,19,128,384]{4,3,2,1,0:T(8,128)(2,1)} %bitcast.98, s32[]{:T(128)S(6)} %select_n.118), kind=kLoop, calls=%fused_computation.7 | loop fusion | flops 14942208 | bytes 22413316 | tf_op jit(solution)/shard_map/convert_element_type | solution.py:77
  136.5 5.5 %dynamic-slice_bitcast_fusion.4 = (bf16[19,128,384]{2,1,0:T(8,128)(2,1)}, bf16[19,128,384]{2,1,0:T(8,128)(2,1)}, bf16[19,128,384]{2,1,0:T(8,128)(2,1)}) fusion(bf16[4,19,128,384]{3,2,1,0:T(8,128)(2,1)} %fusion.2, s32[]{:T(128)S(6)} %select_n.124, s32[]{:T(128)S(6)} %select_n.126, s32[]{:T(128)S(6)} %select_n.125), kind=kLoop, calls=%fused_computation.57 | loop fusion | bytes 11206668 | tf_op jit(solution)/shard_map/jit(dynamic_index_in_dim)/squeeze | solution.py:92
  142.0 2.8 collective-permute-start.1
  144.8 1.5 collective-permute-start.2
  146.4 10.0 %subtract_convert_fusion.1 = (bf16[96,128,128]{2,1,0:T(8,128)(2,1)S(1)}, bf16[96,128,128]{2,1,0:T(8,128)(2,1)}) fusion(bf16[96,128,512]{2,1,0:T(8,128)(2,1)} %reshape.165, f32[96,128]{1,0:T(8,128)S(1)} %bitcast.121, s32[96,128]{1,0:T(8,128)S(1)} %copy-done.20, f32[96,128]{1,0:T(8,128)S(1)} %bitcast.123, s32[96,128]{1,0:T(8,128)S(1)} %copy-done.22, ...), kind=kOutput, calls=%fused_computation.16 | convolution fusion | flops 446693376 | bytes 10223616 | tf_op jit(solution)/shard_map/bcr,brf->bcf/dot_general | solution.py:62
  156.4 2.4 pad_maximum_fusion.1
  158.9 4.7 %fusion.23 = bf16[152,128,128]{2,0,1:T(8,128)(2,1)S(1)} fusion(bf16[192,128,128]{2,1,0:T(8,128)(2,1)S(1)} %pad_maximum_fusion.1, pred[152,96]{1,0:T(8,128)(4,1)S(1)} %iota_compare_fusion.8), kind=kOutput, calls=%fused_computation.48 | convolution fusion | flops 958820864 | bytes 11286784 | tf_op jit(solution)/shard_map/sb,bcf->scf/dot_general | solution.py:65
  163.6 1.3 copy.32
  164.9 0.1 subtract_multiply_fusion
  165.0 2.0 dynamic-slice_bitcast_fusion.1
  167.0 19.7 %collective-permute-done.1 = bf16[19,128,384]{2,1,0:T(8,128)(2,1)} collective-permute-done((bf16[19,128,384]{2,1,0:T(8,128)(2,1)}, bf16[19,128,384]{2,1,0:T(8,128)(2,1)}, u32[]{:S(2)}, u32[]{:S(2)}) %collective-permute-start.1) | collective-permute-done | bytes 1867808 | tf_op jit(solution)/shard_map/ppermute | solution.py:93
  186.7 40.9 %collective-permute-done.2 = bf16[19,128,384]{2,1,0:T(8,128)(2,1)} collective-permute-done((bf16[19,128,384]{2,1,0:T(8,128)(2,1)}, bf16[19,128,384]{2,1,0:T(8,128)(2,1)}, u32[]{:S(2)}, u32[]{:S(2)}) %collective-permute-start.2) | collective-permute-done | bytes 1867808 | tf_op jit(solution)/shard_map/ppermute | solution.py:93
  227.6 5.2 %fusion.20 = bf16[19,128,384]{2,1,0:T(8,128)(2,1)S(1)} fusion(bf16[19,128,384]{2,1,0:T(8,128)(2,1)} %collective-permute-done.3, bf16[19,128,384]{2,1,0:T(8,128)(2,1)} %collective-permute-done.2, bf16[19,128,384]{2,1,0:T(8,128)(2,1)} %collective-permute-done.1, bf16[4,19,128,384]{3,2,1,0:T(8,128)(2,1)} %collective-permute-done, s32[]{:T(128)S(6)} %select_n.121, ...), kind=kLoop, calls=%fused_computation.44 | loop fusion | flops 9338880 | bytes 11206668 | tf_op jit(solution)/shard_map/convert_element_type | solution.py:97
  232.9 0.1 collective-permute-start.4
  233.0 17.7 %multiply_convert_fusion.1 = (bf16[1024,1024]{1,0:T(8,128)(2,1)S(1)}, bf16[1024,1024]{1,0:T(8,128)(2,1)S(1)}, bf16[1024,1024]{1,0:T(8,128)(2,1)S(1)}) fusion(f32[1024]{0:T(1024)S(1)} %subtract_multiply_fusion), kind=kLoop, calls=%fused_computation.35 | loop fusion | flops 22020096 | bytes 6295552 | tf_op jit(solution)/shard_map/convert.20
  250.7 36.9 %maximum_maximum_fusion = bf16[2048,2048]{1,0:T(8,128)(2,1)} fusion(bf16[1024,1024]{1,0:T(8,128)(2,1)S(1)} %get-tuple-element.36, bf16[1024,1024]{1,0:T(8,128)(2,1)S(1)} %get-tuple-element.35, bf16[1024,1024]{1,0:T(8,128)(2,1)S(1)} %get-tuple-element.34), kind=kLoop, calls=%fused_computation.11 | loop fusion | flops 33554432 | bytes 14680064 | tf_op jit(solution)/shard_map/concatenate | solution.py:43
  287.6 2.6 copy.28
  290.1 5.1 %all-to-all-start = ((bf16[19,128,384]{2,0,1:T(8,128)(2,1)}), bf16[19,128,384]{2,0,1:T(8,128)(2,1)S(1)}, u32[]{:S(2)}, u32[]{:S(2)}) async-start(bf16[19,128,384]{2,0,1:T(8,128)(2,1)} %copy.28), calls=%async_computation | async-start | bytes 4718592 | tf_op jit(solution)/shard_map/all_to_all | solution.py:135
  295.2 0.0 copy-start.3
  295.3 3.6 fusion.10
  298.8 1.3 dynamic-slice_bitcast_fusion.7
  300.1 1.2 collective-permute-start.5
  301.3 0.8 collective-permute-start.6
  302.2 1.4 collective-permute-start.7
  303.6 2.9 convert_element_type.185
  306.5 8.3 %copy.30 = bf16[4,2,256,2048]{3,2,1,0:T(8,128)(2,1)} copy(bf16[4,2,256,2048]{3,2,0,1:T(8,128)(2,1)} %bitcast.102) | data formatting | bytes 16777216 | tf_op jit(solution)/shard_map/transpose | solution.py:131
  314.8 6.5 %slice.109 = bf16[4,384,2048]{2,1,0:T(8,128)(2,1)} slice(bf16[4,512,2048]{2,1,0:T(8,128)(2,1)} %bitcast.103), slice={[0:4], [0:384], [0:2048]} | slice | bytes 12582912 | tf_op jit(solution)/shard_map/slice | solution.py:137
  321.4 3.2 slice.111
  324.5 25.1 %all-to-all-done = bf16[19,128,384]{2,0,1:T(8,128)(2,1)S(1)} async-done(((bf16[19,128,384]{2,0,1:T(8,128)(2,1)}), bf16[19,128,384]{2,0,1:T(8,128)(2,1)S(1)}, u32[]{:S(2)}, u32[]{:S(2)}) %all-to-all-start) | async-done | bytes 1867808 | tf_op jit(solution)/shard_map/all_to_all | solution.py:135
  349.6 1.5 copy.29
  351.1 1.7 copy.35
  352.8 2.1 fusion.32
  354.9 1.3 copy.33
  356.3 3.7 all-to-all-start.1
  360.0 9.8 %fusion.42 = f32[608,2048]{1,0:T(8,128)} fusion(bf16[608,1536]{1,0:T(8,128)(2,1)} %bitcast.116, bf16[1536,2048]{1,0:T(8,128)(2,1)} %bitcast.113), kind=kOutput, calls=%fused_computation.104 | convolution fusion | flops 3825205248 | bytes 13139968 | tf_op jit(solution)/shard_map/dot_general | solution.py:138
  369.8 10.0 %all-to-all-done.1 = bf16[19,128,128]{2,0,1:T(8,128)(2,1)S(1)} async-done(((bf16[19,128,128]{2,0,1:T(8,128)(2,1)}), bf16[19,128,128]{2,0,1:T(8,128)(2,1)S(1)}, u32[]{:S(2)}, u32[]{:S(2)}) %all-to-all-start.1) | async-done | bytes 622624 | tf_op jit(solution)/shard_map/all_to_all | solution.py:135
  379.8 0.5 copy.34
  380.3 4.1 %convolution_add_fusion = f32[608,2048]{1,0:T(8,128)S(1)} fusion(f32[608,2048]{1,0:T(8,128)} %fusion.42, bf16[512,2048]{1,0:T(8,128)(2,1)S(1)} %bitcast.111, bf16[76,8,4,128]{3,2,1,0:T(4,128)(2,1)S(1)} %bitcast.114), kind=kOutput, calls=%fused_computation.45 | convolution fusion | flops 1276313600 | bytes 12681216 | tf_op jit(solution)/shard_map/dot_general | solution.py:138
  384.5 1.3 fusion.27
  385.8 0.1 collective-permute-start.8
  385.9 4.6 %collective-permute-done.8 = f32[19,1024]{1,0:T(8,128)S(1)} collective-permute-done((f32[19,1024]{1,0:T(8,128)S(1)}, f32[19,1024]{1,0:T(8,128)S(1)}, u32[]{:S(2)}, u32[]{:S(2)}) %collective-permute-start.8) | collective-permute-done | bytes 77856 | tf_op jit(solution)/shard_map/ppermute | solution.py:55
  390.5 0.1 collective-permute-start.9
  390.6 1.8 convert_element_type.184
  392.4 4.2 %collective-permute-done.9 = f32[19,1024]{1,0:T(8,128)S(1)} collective-permute-done((f32[19,1024]{1,0:T(8,128)S(1)}, f32[19,1024]{1,0:T(8,128)S(1)}, u32[]{:S(2)}, u32[]{:S(2)}) %collective-permute-start.9) | collective-permute-done | bytes 77856 | tf_op jit(solution)/shard_map/ppermute | solution.py:55
  396.6 0.7 add_multiply_fusion
  (60 shorter events, 0.2 us)
Async XLA Ops:
  4.7 28.6 %copy-start.5 = (f32[96,1,128]{2,1,0:T(1,128)}, f32[96,1,128]{2,1,0:T(1,128)S(1)}, u32[]{:S(2)}) copy-start(f32[96,1,128]{2,1,0:T(1,128)S(1)} %get-tuple-element.25) | copy-start | bytes 147460
  4.7 20.5 %copy-start.23 = (s32[96]{0:T(128)S(1)}, s32[96]{0:T(128)}, u32[]{:S(2)}) copy-start(s32[96]{0:T(128)} %param.11) | copy-start | bytes 1156
  4.7 20.5 %copy-start = (s32[80]{0:T(128)S(1)}, s32[80]{0:T(128)}, u32[]{:S(2)}) copy-start(s32[80]{0:T(128)} %param.12) | copy-start | bytes 964
  4.7 23.4 %copy-start.4 = (s32[12288]{0:T(1024)S(1)}, s32[12288]{0:T(1024)}, u32[]{:S(2)}) copy-start(s32[12288]{0:T(1024)} %param.8) | copy-start | bytes 147460
  33.2 14.3 %copy-start.7 = (s32[96,128]{1,0:T(8,128)}, s32[96,128]{1,0:T(8,128)S(1)}, u32[]{:S(2)}) copy-start(s32[96,128]{1,0:T(8,128)S(1)} %get-tuple-element.26) | copy-start | bytes 147460
  33.2 14.3 %copy-start.9 = (s32[96,128]{1,0:T(8,128)}, s32[96,128]{1,0:T(8,128)S(1)}, u32[]{:S(2)}) copy-start(s32[96,128]{1,0:T(8,128)S(1)} %get-tuple-element.27) | copy-start | bytes 147460
  33.2 14.2 %copy-start.11 = (s32[96,128]{1,0:T(8,128)}, s32[96,128]{1,0:T(8,128)S(1)}, u32[]{:S(2)}) copy-start(s32[96,128]{1,0:T(8,128)S(1)} %get-tuple-element.28) | copy-start | bytes 147460
  33.2 14.2 %copy-start.13 = (s32[96,128]{1,0:T(8,128)}, s32[96,128]{1,0:T(8,128)S(1)}, u32[]{:S(2)}) copy-start(s32[96,128]{1,0:T(8,128)S(1)} %get-tuple-element.29) | copy-start | bytes 147460
  33.2 14.2 %copy-start.15 = (s32[96,128]{1,0:T(8,128)}, s32[96,128]{1,0:T(8,128)S(1)}, u32[]{:S(2)}) copy-start(s32[96,128]{1,0:T(8,128)S(1)} %get-tuple-element.30) | copy-start | bytes 147460
  33.2 14.2 %copy-start.17 = (s32[96,128]{1,0:T(8,128)}, s32[96,128]{1,0:T(8,128)S(1)}, u32[]{:S(2)}) copy-start(s32[96,128]{1,0:T(8,128)S(1)} %get-tuple-element.31) | copy-start | bytes 147460
  33.2 14.2 %copy-start.19 = (s32[96,128]{1,0:T(8,128)}, s32[96,128]{1,0:T(8,128)S(1)}, u32[]{:S(2)}) copy-start(s32[96,128]{1,0:T(8,128)S(1)} %get-tuple-element.32) | copy-start | bytes 147460
  33.3 14.2 %copy-start.21 = (s32[96,128]{1,0:T(8,128)}, s32[96,128]{1,0:T(8,128)S(1)}, u32[]{:S(2)}) copy-start(s32[96,128]{1,0:T(8,128)S(1)} %get-tuple-element.33) | copy-start | bytes 147460
  112.2 12.3 %collective-permute-start = (bf16[4,19,128,384]{3,2,1,0:T(8,128)(2,1)}, bf16[4,19,128,384]{3,2,1,0:T(8,128)(2,1)}, u32[]{:S(2)}, u32[]{:S(2)}) collective-permute-start(bf16[4,19,128,384]{3,2,1,0:T(8,128)(2,1)} %dynamic-slice_bitcast_fusion), channel_id=1, source_target_pairs={{0,4},{4,0},{8,12},{12,8},{16,20},{20,16},{24,28},{28,24},{1,5},{5... | collective-permute-start | bytes 22413320 | tf_op jit(solution)/shard_map/ppermute | solution.py:76
  136.4 9.9 %copy-start.6 = (f32[96,1,128]{2,1,0:T(1,128)S(1)}, f32[96,1,128]{2,1,0:T(1,128)}, u32[]{:S(2)}) copy-start(f32[96,1,128]{2,1,0:T(1,128)} %copy-done.5) | copy-start | bytes 147460
  136.4 9.9 %copy-start.8 = (s32[96,128]{1,0:T(8,128)S(1)}, s32[96,128]{1,0:T(8,128)}, u32[]{:S(2)}) copy-start(s32[96,128]{1,0:T(8,128)} %copy-done.7) | copy-start | bytes 147460
  136.4 9.9 %copy-start.10 = (s32[96,128]{1,0:T(8,128)S(1)}, s32[96,128]{1,0:T(8,128)}, u32[]{:S(2)}) copy-start(s32[96,128]{1,0:T(8,128)} %copy-done.9) | copy-start | bytes 147460
  136.4 9.9 %copy-start.12 = (s32[96,128]{1,0:T(8,128)S(1)}, s32[96,128]{1,0:T(8,128)}, u32[]{:S(2)}) copy-start(s32[96,128]{1,0:T(8,128)} %copy-done.11) | copy-start | bytes 147460
  136.4 9.9 %copy-start.14 = (s32[96,128]{1,0:T(8,128)S(1)}, s32[96,128]{1,0:T(8,128)}, u32[]{:S(2)}) copy-start(s32[96,128]{1,0:T(8,128)} %copy-done.13) | copy-start | bytes 147460
  136.4 9.9 %copy-start.16 = (s32[96,128]{1,0:T(8,128)S(1)}, s32[96,128]{1,0:T(8,128)}, u32[]{:S(2)}) copy-start(s32[96,128]{1,0:T(8,128)} %copy-done.15) | copy-start | bytes 147460
  136.4 9.9 %copy-start.18 = (s32[96,128]{1,0:T(8,128)S(1)}, s32[96,128]{1,0:T(8,128)}, u32[]{:S(2)}) copy-start(s32[96,128]{1,0:T(8,128)} %copy-done.17) | copy-start | bytes 147460
  136.5 9.9 %copy-start.20 = (s32[96,128]{1,0:T(8,128)S(1)}, s32[96,128]{1,0:T(8,128)}, u32[]{:S(2)}) copy-start(s32[96,128]{1,0:T(8,128)} %copy-done.19) | copy-start | bytes 147460
  136.5 9.9 %copy-start.22 = (s32[96,128]{1,0:T(8,128)S(1)}, s32[96,128]{1,0:T(8,128)}, u32[]{:S(2)}) copy-start(s32[96,128]{1,0:T(8,128)} %copy-done.21) | copy-start | bytes 147460
  142.0 44.7 %collective-permute-start.1 = (bf16[19,128,384]{2,1,0:T(8,128)(2,1)}, bf16[19,128,384]{2,1,0:T(8,128)(2,1)}, u32[]{:S(2)}, u32[]{:S(2)}) collective-permute-start(bf16[19,128,384]{2,1,0:T(8,128)(2,1)} %get-tuple-element.12), channel_id=1, source_target_pairs={{0,8},{4,12},{8,0},{12,4},{16,24},{20,28},{24,16},{28,20},{1,9},{5... | collective-permute-start | bytes 5603336 | tf_op jit(solution)/shard_map/ppermute | solution.py:93
  144.8 82.8 %collective-permute-start.2 = (bf16[19,128,384]{2,1,0:T(8,128)(2,1)}, bf16[19,128,384]{2,1,0:T(8,128)(2,1)}, u32[]{:S(2)}, u32[]{:S(2)}) collective-permute-start(bf16[19,128,384]{2,1,0:T(8,128)(2,1)} %get-tuple-element.14), channel_id=1, source_target_pairs={{0,16},{4,20},{8,24},{12,28},{16,0},{20,4},{24,8},{28,12},{1,17},{... | collective-permute-start | bytes 5603336 | tf_op jit(solution)/shard_map/ppermute | solution.py:93
  146.3 81.3 %collective-permute-start.3 = (bf16[19,128,384]{2,1,0:T(8,128)(2,1)}, bf16[19,128,384]{2,1,0:T(8,128)(2,1)}, u32[]{:S(2)}, u32[]{:S(2)}) collective-permute-start(bf16[19,128,384]{2,1,0:T(8,128)(2,1)} %get-tuple-element.13), channel_id=1, source_target_pairs={{0,24},{4,28},{8,16},{12,20},{16,8},{20,12},{24,0},{28,4},{1,25},{... | collective-permute-start | bytes 5603336 | tf_op jit(solution)/shard_map/ppermute | solution.py:93
  164.9 68.0 %copy-start.1 = (bf16[152,128,128]{2,1,0:T(8,128)(2,1)}, bf16[152,128,128]{2,1,0:T(8,128)(2,1)S(1)}, u32[]{:S(2)}) copy-start(bf16[152,128,128]{2,1,0:T(8,128)(2,1)S(1)} %copy.32) | copy-start | bytes 14942212
  232.9 62.4 %collective-permute-start.4 = (bf16[4,19,128,128]{3,2,1,0:T(8,128)(2,1)}, bf16[4,19,128,128]{3,2,1,0:T(8,128)(2,1)}, u32[]{:S(2)}, u32[]{:S(2)}) collective-permute-start(bf16[4,19,128,128]{3,2,1,0:T(8,128)(2,1)} %dynamic-slice_bitcast_fusion.1), channel_id=1, source_target_pairs={{0,4},{4,0},{8,12},{12,8},{16,20},{20,16},{24,28},{28,24},{1,5},{5... | collective-permute-start | bytes 7471112 | tf_op jit(solution)/shard_map/ppermute | solution.py:76
  290.1 59.5 %all-to-all-start = ((bf16[19,128,384]{2,0,1:T(8,128)(2,1)}), bf16[19,128,384]{2,0,1:T(8,128)(2,1)S(1)}, u32[]{:S(2)}, u32[]{:S(2)}) async-start(bf16[19,128,384]{2,0,1:T(8,128)(2,1)} %copy.28), calls=%async_computation | async-start | bytes 4718592 | tf_op jit(solution)/shard_map/all_to_all | solution.py:135
  295.2 8.4 %copy-start.3 = (bf16[19,32,2048]{2,1,0:T(8,128)(2,1)S(1)}, bf16[19,32,2048]{2,1,0:T(8,128)(2,1)}, u32[]{:S(2)}) copy-start(bf16[19,32,2048]{2,1,0:T(8,128)(2,1)} %param.13) | copy-start | bytes 7471108
  300.1 52.7 %collective-permute-start.5 = (bf16[19,128,128]{2,1,0:T(8,128)(2,1)}, bf16[19,128,128]{2,1,0:T(8,128)(2,1)S(1)}, u32[]{:S(2)}, u32[]{:S(2)}) collective-permute-start(bf16[19,128,128]{2,1,0:T(8,128)(2,1)} %get-tuple-element.15), channel_id=1, source_target_pairs={{0,8},{4,12},{8,0},{12,4},{16,24},{20,28},{24,16},{28,20},{1,9},{5... | collective-permute-start | bytes 1867784 | tf_op jit(solution)/shard_map/ppermute | solution.py:93
  301.3 51.4 %collective-permute-start.6 = (bf16[19,128,128]{2,1,0:T(8,128)(2,1)}, bf16[19,128,128]{2,1,0:T(8,128)(2,1)}, u32[]{:S(2)}, u32[]{:S(2)}) collective-permute-start(bf16[19,128,128]{2,1,0:T(8,128)(2,1)} %get-tuple-element.17), channel_id=1, source_target_pairs={{0,16},{4,20},{8,24},{12,28},{16,0},{20,4},{24,8},{28,12},{1,17},{... | collective-permute-start | bytes 1867784 | tf_op jit(solution)/shard_map/ppermute | solution.py:93
  302.2 50.6 %collective-permute-start.7 = (bf16[19,128,128]{2,1,0:T(8,128)(2,1)}, bf16[19,128,128]{2,1,0:T(8,128)(2,1)}, u32[]{:S(2)}, u32[]{:S(2)}) collective-permute-start(bf16[19,128,128]{2,1,0:T(8,128)(2,1)} %get-tuple-element.16), channel_id=1, source_target_pairs={{0,24},{4,28},{8,16},{12,20},{16,8},{20,12},{24,0},{28,4},{1,25},{... | collective-permute-start | bytes 1867784 | tf_op jit(solution)/shard_map/ppermute | solution.py:93
  356.3 23.5 %all-to-all-start.1 = ((bf16[19,128,128]{2,0,1:T(8,128)(2,1)}), bf16[19,128,128]{2,0,1:T(8,128)(2,1)S(1)}, u32[]{:S(2)}, u32[]{:S(2)}) async-start(bf16[19,128,128]{2,0,1:T(8,128)(2,1)} %copy.33), calls=%async_computation.1 | async-start | bytes 1572864 | tf_op jit(solution)/shard_map/all_to_all | solution.py:135
  360.0 20.3 %copy-start.2 = (bf16[4,128,2048]{2,1,0:T(8,128)(2,1)S(1)}, bf16[4,128,2048]{2,1,0:T(8,128)(2,1)}, u32[]{:S(2)}) copy-start(bf16[4,128,2048]{2,1,0:T(8,128)(2,1)} %slice.111) | copy-start | bytes 6291460
  379.8 4.7 %slice-start = ((s8[4980736]{0:T(1024)(128)(4,1)}), s8[4194304]{0:T(1024)(128)(4,1)S(1)}, s32[]{:S(2)}) async-start(s8[4980736]{0:T(1024)(128)(4,1)} %bitcast.108), calls=%async_computation.2 | async-start | bytes 8388608
  380.3 4.2 %slice-start.1 = ((s8[4980736]{0:T(1024)(128)(4,1)}), s8[786432]{0:T(1024)(128)(4,1)S(1)}, s32[]{:S(2)}) async-start(s8[4980736]{0:T(1024)(128)(4,1)} %bitcast.108), calls=%async_computation.3 | async-start | bytes 1572864
  385.8 4.7 %collective-permute-start.8 = (f32[19,1024]{1,0:T(8,128)S(1)}, f32[19,1024]{1,0:T(8,128)S(1)}, u32[]{:S(2)}, u32[]{:S(2)}) collective-permute-start(f32[19,1024]{1,0:T(8,128)S(1)} %fusion.27), channel_id=1, source_target_pairs={{0,1},{1,0},{2,3},{3,2},{4,5},{5,4},{6,7},{7,6},{8,9},{9,8},{10,11... | collective-permute-start | bytes 233480 | tf_op jit(solution)/shard_map/ppermute | solution.py:55
  390.5 6.1 %collective-permute-start.9 = (f32[19,1024]{1,0:T(8,128)S(1)}, f32[19,1024]{1,0:T(8,128)S(1)}, u32[]{:S(2)}, u32[]{:S(2)}) collective-permute-start(f32[19,1024]{1,0:T(8,128)S(1)} %add.327), channel_id=1, source_target_pairs={{0,2},{1,3},{2,0},{3,1},{4,6},{5,7},{6,4},{7,5},{8,10},{9,11},{10,... | collective-permute-start | bytes 233480 | tf_op jit(solution)/shard_map/ppermute | solution.py:55
where the time goes:
time: 404 us; the launch traced here: 398 us
  waiting for transfers between devices  116 us (29%)
  other arithmetic  110 us (27%)
  local copies, waits for them, and re-layouts  79.8 us (20%)
  matrix products  72.8 us (18%)
  starting transfers between devices  17.4 us (4%)
    ppermute x6, waiting for transfers between devices, _scatter_pairs(): lax.ppermute(send, 'uv', _partner_pairs(n_owners, lambda i, dest=dest: de...  60.7 us
    concatenate x1, other arithmetic, delay_table(): return jnp.concatenate([upper, lower], axis=0).astype(jnp.bfloat16)  36.9 us
    all_to_all x2, waiting for transfers between devices, body(): lax.all_to_all(gridded, 'chan', split_axis=1, concat_axis=2, tiled=True)  35.1 us
    dot_general x2, matrix products, _gather_pair(): jnp.einsum('sb,bcf->scf', pick2, jnp.concatenate([high, low], axis=0), pr...  34.7 us
    dot_general x2, matrix products, _gather_pair(): jnp.einsum('bcr,brf->bcf', matrix, part, preferred_element_type=jnp.float32)  24.2 us
    reshape x1, local copies, waits for them, and re-layouts, body(): blocks = vis.reshape(nblocks, BR, width)  20.5 us
    concatenate x2, other arithmetic, _gather_pair(): jnp.concatenate([high, low], axis=0)  17.7 us
    another operation x1, other arithmetic  17.7 us
  transfers between devices with their start and end apart: 12, of which 7 were waited for; matrix products, arithmetic and copies ran while one was open for 30% of the time, Pallas kernels for 0%

commit v1 on v0

--- a/solution.py
+++ b/solution.py
@@ -132,7 +132,12 @@
     by_source = by_source.reshape(n_chan, width, 2 * CH)
     out = None
     for gridded, lo, hi in ((first_grid, 0, cut), (second_grid, cut, width)):
-        piece = lax.all_to_all(gridded, "chan", split_axis=1, concat_axis=2, tiled=True)
+        piece = jnp.concatenate(
+            lax.all_to_all(
+                jnp.stack(jnp.split(gridded, lax.axis_size("chan"), axis=1)), "chan", 0, 0
+            ),
+            axis=2,
+        )
         count, cells_part = (piece.shape[0], piece.shape[1])
         rows = by_source[:, lo:hi, :].reshape(n_chan * (hi - lo), 2 * CH)
         term = jnp.dot(

time: 404 us -> 372 us (0.921)
  waiting for transfers between devices: 116 us -> 86.3 us
  local copies, waits for them, and re-layouts: 79.8 us -> 75.7 us
    ppermute x6, waiting for transfers between devices: 60.7 us -> 43 us  [_scatter_pairs(): lax.ppermute(send, 'uv', _partner_pairs(n_owners, lambda i, dest=dest: de...]
    all_to_all x2, waiting for transfers between devices: 35.1 us -> 22.7 us  [body(): lax.all_to_all(jnp.stack(jnp.split(gridded, lax.axis_size('chan'), axis=1...]
    another operation x1 -> x3, other arithmetic: 17.7 us -> 20.1 us
  transfers between devices with their start and end apart: 12 -> 12, of which waited for: 7 -> 7; matrix products, arithmetic and copies ran while one was open for 30% -> 32% of each run, Pallas kernels for 0% -> 0%
where the time goes in v1:
time: 372 us; the launch traced here: 366 us
  other arithmetic  113 us (30%)
  waiting for transfers between devices  86.3 us (23%)
  local copies, waits for them, and re-layouts  75.7 us (20%)
  matrix products  72.6 us (20%)
  starting transfers between devices  17.1 us (5%)
    ppermute x6, waiting for transfers between devices, _scatter_pairs(): lax.ppermute(send, 'uv', _partner_pairs(n_owners, lambda i, dest=dest: de...  43 us
    concatenate x1, other arithmetic, delay_table(): return jnp.concatenate([upper, lower], axis=0).astype(jnp.bfloat16)  36.8 us
    dot_general x2, matrix products, _gather_pair(): jnp.einsum('sb,bcf->scf', pick2, jnp.concatenate([high, low], axis=0), pr...  34.7 us
    dot_general x2, matrix products, _gather_pair(): jnp.einsum('bcr,brf->bcf', matrix, part, preferred_element_type=jnp.float32)  24.2 us
    all_to_all x2, waiting for transfers between devices, body(): lax.all_to_all(jnp.stack(jnp.split(gridded, lax.axis_size('chan'), axis=1...  22.7 us
    reshape x1, local copies, waits for them, and re-layouts, body(): blocks = vis.reshape(nblocks, BR, width)  20.5 us
    concatenate x2, other arithmetic, _gather_pair(): jnp.concatenate([high, low], axis=0)  18 us
    another operation x1, other arithmetic  17.6 us
  transfers between devices with their start and end apart: 12, of which 7 were waited for; matrix products, arithmetic and copies ran while one was open for 32% of the time, Pallas kernels for 0%

profile of v1, /device:TPU:0, one launch (start us, length us, event | category | flops | bytes accessed | tf_op | source)
XLA Modules:
  0.0 365.6 jit_solution(5586144388246204806)
XLA Ops:
  0.6 1.6 fusion.41
  2.3 2.4 slice_convert_fusion.7
  4.7 0.0 copy-start.4
  4.7 20.5 %reshape.163 = bf16[96,128,512]{2,1,0:T(8,128)(2,1)} reshape(bf16[12288,2,256]{2,1,0:T(2,128)(2,1)} %param.7) | data formatting | bytes 25165824 | tf_op jit(solution)/shard_map/reshape | solution.py:118
  25.2 0.1 fusion.35
  25.3 0.1 reduce_window_sum.11
  25.4 0.2 select_reduce_fusion
  25.6 1.2 gather_fusion
  26.8 1.2 gather_fusion.1
  28.1 5.1 %add_bitcast_fusion.10 = (s32[96,128]{1,0:T(8,128)S(1)}, s32[96,128]{1,0:T(8,128)S(1)}, s32[96,128]{1,0:T(8,128)S(1)}, s32[96,128]{1,0:T(8,128)S(1)}, s32[96,128...) fusion(s32[12288]{0:T(1024)S(1)} %copy-done.4, s32[]{:T(128)} %bitcast.1, ...), kind=kLoop, calls=%fused_computation.96 | loop fusion | flops 98304 | bytes 442400 | tf_op jit(solution)/shard_map/add | solution.py:23
  33.3 0.0 copy-start.19
  33.3 14.2 %subtract_convert_fusion = (bf16[96,128,384]{2,1,0:T(8,128)(2,1)}, bf16[96,128,384]{2,1,0:T(8,128)(2,1)}) fusion(bf16[96,128,512]{2,1,0:T(8,128)(2,1)} %reshape.163, f32[96,128]{1,0:T(8,128)S(1)} %bitcast.133, s32[96,128]{1,0:T(8,128)S(1)} %get-tuple-element.40, f32[96,128]{1,0:T(8,128)S(1)} %bitcast.135, s32[96,128]{1,0:T(8,128)S(1)} %get-tuple-element.41, ...), kind=kOutput, calls=%fused_computation.5 | convolution fusion | flops 1264582656 | bytes 29097984 | tf_op jit(solution)/shard_map/bcr,brf->bcf/dot_general | solution.py:62
  47.5 15.5 %pad_maximum_fusion = bf16[192,128,384]{2,1,0:T(8,128)(2,1)} fusion(bf16[96,128,384]{2,1,0:T(8,128)(2,1)} %get-tuple-element.10, bf16[96,128,384]{2,1,0:T(8,128)(2,1)} %get-tuple-element.11), kind=kLoop, calls=%fused_computation.2 | loop fusion | flops 9437184 | bytes 37748736 | tf_op jit(solution)/shard_map/concatenate | solution.py:68
  63.1 30.0 %fusion.3 = bf16[152,128,384]{2,0,1:T(8,128)(2,1)} fusion(bf16[192,128,384]{2,1,0:T(8,128)(2,1)} %pad_maximum_fusion, pred[152,96]{1,0:T(8,128)(4,1)S(1)} %iota_compare_fusion.8), kind=kOutput, calls=%fused_computation.8 | convolution fusion | flops 2876404224 | bytes 33831168 | tf_op jit(solution)/shard_map/sb,bcf->scf/dot_general | solution.py:65
  93.0 12.0 %copy.20 = bf16[152,128,384]{2,1,0:T(8,128)(2,1)} copy(bf16[152,128,384]{2,0,1:T(8,128)(2,1)} %fusion.3) | data formatting | bytes 29884416 | tf_op jit(solution)/shard_map/convert_element_type | solution.py:70
  105.1 7.6 %dynamic-slice_bitcast_fusion = bf16[4,19,128,384]{3,2,1,0:T(8,128)(2,1)} fusion(bf16[2,4,19,128,384]{4,3,2,1,0:T(8,128)(2,1)} %bitcast.111, s32[]{:T(128)S(6)} %select_n.123), kind=kLoop, calls=%fused_computation.12 | loop fusion | bytes 14942212 | tf_op jit(solution)/shard_map/jit(dynamic_index_in_dim)/squeeze | solution.py:73
  112.6 0.5 collective-permute-start
  113.1 11.8 %collective-permute-done = bf16[4,19,128,384]{3,2,1,0:T(8,128)(2,1)} collective-permute-done((bf16[4,19,128,384]{3,2,1,0:T(8,128)(2,1)}, bf16[4,19,128,384]{3,2,1,0:T(8,128)(2,1)}, u32[]{:S(2)}, u32[]{:S(2)}) %collective-permute-start) | collective-permute-done | bytes 7471136 | tf_op jit(solution)/shard_map/ppermute | solution.py:76
  125.0 11.9 %fusion.2 = bf16[4,19,128,384]{3,2,1,0:T(8,128)(2,1)} fusion(bf16[4,19,128,384]{3,2,1,0:T(8,128)(2,1)} %collective-permute-done, bf16[2,4,19,128,384]{4,3,2,1,0:T(8,128)(2,1)} %bitcast.112, s32[]{:T(128)S(6)} %select_n.118), kind=kLoop, calls=%fused_computation.7 | loop fusion | flops 14942208 | bytes 22413316 | tf_op jit(solution)/shard_map/convert_element_type | solution.py:77
  136.9 0.0 copy-start.22
  136.9 5.5 %dynamic-slice_bitcast_fusion.4 = (bf16[19,128,384]{2,1,0:T(8,128)(2,1)}, bf16[19,128,384]{2,1,0:T(8,128)(2,1)}, bf16[19,128,384]{2,1,0:T(8,128)(2,1)}) fusion(bf16[4,19,128,384]{3,2,1,0:T(8,128)(2,1)} %fusion.2, s32[]{:T(128)S(6)} %select_n.124, s32[]{:T(128)S(6)} %select_n.126, s32[]{:T(128)S(6)} %select_n.125), kind=kLoop, calls=%fused_computation.58 | loop fusion | bytes 11206668 | tf_op jit(solution)/shard_map/jit(dynamic_index_in_dim)/squeeze | solution.py:92
  142.4 2.8 collective-permute-start.1
  145.2 1.5 collective-permute-start.2
  146.8 10.0 %subtract_convert_fusion.1 = (bf16[96,128,128]{2,1,0:T(8,128)(2,1)S(1)}, bf16[96,128,128]{2,1,0:T(8,128)(2,1)}) fusion(bf16[96,128,512]{2,1,0:T(8,128)(2,1)} %reshape.163, f32[96,128]{1,0:T(8,128)S(1)} %bitcast.134, s32[96,128]{1,0:T(8,128)S(1)} %copy-done.20, f32[96,128]{1,0:T(8,128)S(1)} %bitcast.136, s32[96,128]{1,0:T(8,128)S(1)} %copy-done.22, ...), kind=kOutput, calls=%fused_computation.16 | convolution fusion | flops 446693376 | bytes 10223616 | tf_op jit(solution)/shard_map/bcr,brf->bcf/dot_general | solution.py:62
  156.9 2.4 pad_maximum_fusion.1
  159.3 4.7 %fusion.23 = bf16[152,128,128]{2,0,1:T(8,128)(2,1)S(1)} fusion(bf16[192,128,128]{2,1,0:T(8,128)(2,1)S(1)} %pad_maximum_fusion.1, pred[152,96]{1,0:T(8,128)(4,1)S(1)} %iota_compare_fusion.8), kind=kOutput, calls=%fused_computation.48 | convolution fusion | flops 958820864 | bytes 11286784 | tf_op jit(solution)/shard_map/sb,bcf->scf/dot_general | solution.py:65
  164.0 1.3 copy.24
  165.4 0.1 subtract_multiply_fusion
  165.4 2.0 dynamic-slice_bitcast_fusion.1
  167.4 17.6 %multiply_convert_fusion.1 = (bf16[1024,1024]{1,0:T(8,128)(2,1)S(1)}, bf16[1024,1024]{1,0:T(8,128)(2,1)S(1)}, bf16[1024,1024]{1,0:T(8,128)(2,1)S(1)}) fusion(f32[1024]{0:T(1024)S(1)} %subtract_multiply_fusion), kind=kLoop, calls=%fused_computation.35 | loop fusion | flops 22020096 | bytes 6295552 | tf_op jit(solution)/shard_map/convert.20
  185.1 2.1 collective-permute-done.1
  187.1 40.9 %collective-permute-done.2 = bf16[19,128,384]{2,1,0:T(8,128)(2,1)} collective-permute-done((bf16[19,128,384]{2,1,0:T(8,128)(2,1)}, bf16[19,128,384]{2,1,0:T(8,128)(2,1)}, u32[]{:S(2)}, u32[]{:S(2)}) %collective-permute-start.2) | collective-permute-done | bytes 1867808 | tf_op jit(solution)/shard_map/ppermute | solution.py:93
  228.1 5.3 %fusion.20 = bf16[19,128,384]{2,1,0:T(8,128)(2,1)S(1)} fusion(bf16[19,128,384]{2,1,0:T(8,128)(2,1)} %collective-permute-done.3, bf16[19,128,384]{2,1,0:T(8,128)(2,1)} %collective-permute-done.2, bf16[19,128,384]{2,1,0:T(8,128)(2,1)} %collective-permute-done.1, bf16[4,19,128,384]{3,2,1,0:T(8,128)(2,1)} %collective-permute-done, s32[]{:T(128)S(6)} %select_n.121, ...), kind=kLoop, calls=%fused_computation.44 | loop fusion | flops 9338880 | bytes 11206668 | tf_op jit(solution)/shard_map/convert_element_type | solution.py:97
  233.4 0.1 collective-permute-start.4
  233.5 36.8 %maximum_maximum_fusion = bf16[2048,2048]{1,0:T(8,128)(2,1)} fusion(bf16[1024,1024]{1,0:T(8,128)(2,1)S(1)} %get-tuple-element.44, bf16[1024,1024]{1,0:T(8,128)(2,1)S(1)} %get-tuple-element.43, bf16[1024,1024]{1,0:T(8,128)(2,1)S(1)} %get-tuple-element.42), kind=kLoop, calls=%fused_computation.11 | loop fusion | flops 33554432 | bytes 14680064 | tf_op jit(solution)/shard_map/concatenate | solution.py:43
  270.3 0.2 slice_bitcast_fusion.3
  270.5 1.5 pad_maximum_fusion.2
  272.0 5.1 %all-to-all-start = ((bf16[4,19,32,384]{3,2,1,0:T(8,128)(2,1)}), bf16[4,19,32,384]{3,2,1,0:T(8,128)(2,1)}, u32[]{:S(2)}, u32[]{:S(2)}) async-start(bf16[4,19,32,384]{3,2,1,0:T(8,128)(2,1)} %pad_maximum_fusion.2), calls=%async_computation | async-start | bytes 3735552 | tf_op jit(solution)/shard_map/all_to_all | solution.py:136
  277.1 3.6 fusion.10
  280.7 1.3 dynamic-slice_bitcast_fusion.7
  282.0 1.2 collective-permute-start.5
  283.3 0.8 collective-permute-start.6
  284.1 1.4 collective-permute-start.7
  285.5 2.9 convert_element_type.185
  288.5 8.3 %copy.22 = bf16[4,2,256,2048]{3,2,1,0:T(8,128)(2,1)} copy(bf16[4,2,256,2048]{3,2,0,1:T(8,128)(2,1)} %bitcast.116) | data formatting | bytes 16777216 | tf_op jit(solution)/shard_map/transpose | solution.py:131
  296.7 6.6 %slice.109 = bf16[4,384,2048]{2,1,0:T(8,128)(2,1)} slice(bf16[4,512,2048]{2,1,0:T(8,128)(2,1)} %bitcast.117), slice={[0:4], [0:384], [0:2048]} | slice | bytes 12582912 | tf_op jit(solution)/shard_map/slice | solution.py:142
  303.3 1.7 slice.111
  305.0 16.1 %all-to-all-done = bf16[4,19,32,384]{3,2,1,0:T(8,128)(2,1)} async-done(((bf16[4,19,32,384]{3,2,1,0:T(8,128)(2,1)}), bf16[4,19,32,384]{3,2,1,0:T(8,128)(2,1)}, u32[]{:S(2)}, u32[]{:S(2)}) %all-to-all-start) | async-done | bytes 1867808 | tf_op jit(solution)/shard_map/all_to_all | solution.py:136
  321.1 2.5 copy.21
  323.6 1.7 copy.26
  325.3 2.1 fusion.32
  327.5 0.9 pad_maximum_fusion.3
  328.4 3.5 all-to-all-start.1
  331.9 9.7 %fusion.42 = f32[608,2048]{1,0:T(8,128)} fusion(bf16[608,1536]{1,0:T(8,128)(2,1)} %bitcast.129, bf16[1536,2048]{1,0:T(8,128)(2,1)} %bitcast.126), kind=kOutput, calls=%fused_computation.114 | convolution fusion | flops 3825205248 | bytes 13139968 | tf_op jit(solution)/shard_map/dot_general | solution.py:143
  341.5 6.7 %all-to-all-done.1 = bf16[4,19,32,128]{3,2,1,0:T(8,128)(2,1)S(1)} async-done(((bf16[4,19,32,128]{3,2,1,0:T(8,128)(2,1)}), bf16[4,19,32,128]{3,2,1,0:T(8,128)(2,1)S(1)}, u32[]{:S(2)}, u32[]{:S(2)}) %all-to-all-start.1) | async-done | bytes 622624 | tf_op jit(solution)/shard_map/all_to_all | solution.py:136
  348.2 0.3 copy.25
  348.5 4.0 %convolution_add_fusion = f32[608,2048]{1,0:T(8,128)S(1)} fusion(f32[608,2048]{1,0:T(8,128)} %fusion.42, bf16[512,2048]{1,0:T(8,128)(2,1)S(1)} %bitcast.124, bf16[76,8,4,128]{3,2,1,0:T(4,128)(2,1)S(1)} %bitcast.127), kind=kOutput, calls=%fused_computation.45 | convolution fusion | flops 1276313600 | bytes 12681216 | tf_op jit(solution)/shard_map/dot_general | solution.py:143
  352.6 1.3 fusion.27
  354.0 0.1 collective-permute-start.8
  354.0 4.6 %collective-permute-done.8 = f32[19,1024]{1,0:T(8,128)S(1)} collective-permute-done((f32[19,1024]{1,0:T(8,128)S(1)}, f32[19,1024]{1,0:T(8,128)S(1)}, u32[]{:S(2)}, u32[]{:S(2)}) %collective-permute-start.8) | collective-permute-done | bytes 77856 | tf_op jit(solution)/shard_map/ppermute | solution.py:55
  358.7 0.1 collective-permute-start.9
  358.7 1.8 convert_element_type.184
  360.6 4.2 %collective-permute-done.9 = f32[19,1024]{1,0:T(8,128)S(1)} collective-permute-done((f32[19,1024]{1,0:T(8,128)S(1)}, f32[19,1024]{1,0:T(8,128)S(1)}, u32[]{:S(2)}, u32[]{:S(2)}) %collective-permute-start.9) | collective-permute-done | bytes 77856 | tf_op jit(solution)/shard_map/ppermute | solution.py:55
  364.7 0.7 add_multiply_fusion
  (62 shorter events, 0.2 us)
Async XLA Ops:
  4.7 28.6 %copy-start.5 = (f32[96,1,128]{2,1,0:T(1,128)}, f32[96,1,128]{2,1,0:T(1,128)S(1)}, u32[]{:S(2)}) copy-start(f32[96,1,128]{2,1,0:T(1,128)S(1)} %get-tuple-element.33) | copy-start | bytes 147460
  4.7 20.5 %copy-start.23 = (s32[96]{0:T(128)S(1)}, s32[96]{0:T(128)}, u32[]{:S(2)}) copy-start(s32[96]{0:T(128)} %param.11) | copy-start | bytes 1156
  4.7 20.5 %copy-start = (s32[80]{0:T(128)S(1)}, s32[80]{0:T(128)}, u32[]{:S(2)}) copy-start(s32[80]{0:T(128)} %param.12) | copy-start | bytes 964
  4.7 23.4 %copy-start.4 = (s32[12288]{0:T(1024)S(1)}, s32[12288]{0:T(1024)}, u32[]{:S(2)}) copy-start(s32[12288]{0:T(1024)} %param.8) | copy-start | bytes 147460
  33.2 14.3 %copy-start.7 = (s32[96,128]{1,0:T(8,128)}, s32[96,128]{1,0:T(8,128)S(1)}, u32[]{:S(2)}) copy-start(s32[96,128]{1,0:T(8,128)S(1)} %get-tuple-element.34) | copy-start | bytes 147460
  33.2 14.2 %copy-start.9 = (s32[96,128]{1,0:T(8,128)}, s32[96,128]{1,0:T(8,128)S(1)}, u32[]{:S(2)}) copy-start(s32[96,128]{1,0:T(8,128)S(1)} %get-tuple-element.35) | copy-start | bytes 147460
  33.2 14.2 %copy-start.11 = (s32[96,128]{1,0:T(8,128)}, s32[96,128]{1,0:T(8,128)S(1)}, u32[]{:S(2)}) copy-start(s32[96,128]{1,0:T(8,128)S(1)} %get-tuple-element.36) | copy-start | bytes 147460
  33.2 14.2 %copy-start.13 = (s32[96,128]{1,0:T(8,128)}, s32[96,128]{1,0:T(8,128)S(1)}, u32[]{:S(2)}) copy-start(s32[96,128]{1,0:T(8,128)S(1)} %get-tuple-element.37) | copy-start | bytes 147460
  33.2 14.2 %copy-start.15 = (s32[96,128]{1,0:T(8,128)}, s32[96,128]{1,0:T(8,128)S(1)}, u32[]{:S(2)}) copy-start(s32[96,128]{1,0:T(8,128)S(1)} %get-tuple-element.38) | copy-start | bytes 147460
  33.3 14.2 %copy-start.17 = (s32[96,128]{1,0:T(8,128)}, s32[96,128]{1,0:T(8,128)S(1)}, u32[]{:S(2)}) copy-start(s32[96,128]{1,0:T(8,128)S(1)} %get-tuple-element.39) | copy-start | bytes 147460
  33.3 14.2 %copy-start.19 = (s32[96,128]{1,0:T(8,128)}, s32[96,128]{1,0:T(8,128)S(1)}, u32[]{:S(2)}) copy-start(s32[96,128]{1,0:T(8,128)S(1)} %get-tuple-element.40) | copy-start | bytes 147460
  33.3 14.2 %copy-start.21 = (s32[96,128]{1,0:T(8,128)}, s32[96,128]{1,0:T(8,128)S(1)}, u32[]{:S(2)}) copy-start(s32[96,128]{1,0:T(8,128)S(1)} %get-tuple-element.41) | copy-start | bytes 147460
  112.6 12.3 %collective-permute-start = (bf16[4,19,128,384]{3,2,1,0:T(8,128)(2,1)}, bf16[4,19,128,384]{3,2,1,0:T(8,128)(2,1)}, u32[]{:S(2)}, u32[]{:S(2)}) collective-permute-start(bf16[4,19,128,384]{3,2,1,0:T(8,128)(2,1)} %dynamic-slice_bitcast_fusion), channel_id=1, source_target_pairs={{0,4},{4,0},{8,12},{12,8},{16,20},{20,16},{24,28},{28,24},{1,5},{5... | collective-permute-start | bytes 22413320 | tf_op jit(solution)/shard_map/ppermute | solution.py:76
  136.9 9.9 %copy-start.6 = (f32[96,1,128]{2,1,0:T(1,128)S(1)}, f32[96,1,128]{2,1,0:T(1,128)}, u32[]{:S(2)}) copy-start(f32[96,1,128]{2,1,0:T(1,128)} %copy-done.5) | copy-start | bytes 147460
  136.9 9.9 %copy-start.8 = (s32[96,128]{1,0:T(8,128)S(1)}, s32[96,128]{1,0:T(8,128)}, u32[]{:S(2)}) copy-start(s32[96,128]{1,0:T(8,128)} %copy-done.7) | copy-start | bytes 147460
  136.9 9.9 %copy-start.10 = (s32[96,128]{1,0:T(8,128)S(1)}, s32[96,128]{1,0:T(8,128)}, u32[]{:S(2)}) copy-start(s32[96,128]{1,0:T(8,128)} %copy-done.9) | copy-start | bytes 147460
  136.9 9.9 %copy-start.12 = (s32[96,128]{1,0:T(8,128)S(1)}, s32[96,128]{1,0:T(8,128)}, u32[]{:S(2)}) copy-start(s32[96,128]{1,0:T(8,128)} %copy-done.11) | copy-start | bytes 147460
  136.9 9.9 %copy-start.14 = (s32[96,128]{1,0:T(8,128)S(1)}, s32[96,128]{1,0:T(8,128)}, u32[]{:S(2)}) copy-start(s32[96,128]{1,0:T(8,128)} %copy-done.13) | copy-start | bytes 147460
  136.9 9.9 %copy-start.16 = (s32[96,128]{1,0:T(8,128)S(1)}, s32[96,128]{1,0:T(8,128)}, u32[]{:S(2)}) copy-start(s32[96,128]{1,0:T(8,128)} %copy-done.15) | copy-start | bytes 147460
  136.9 9.9 %copy-start.18 = (s32[96,128]{1,0:T(8,128)S(1)}, s32[96,128]{1,0:T(8,128)}, u32[]{:S(2)}) copy-start(s32[96,128]{1,0:T(8,128)} %copy-done.17) | copy-start | bytes 147460
  136.9 9.9 %copy-start.20 = (s32[96,128]{1,0:T(8,128)S(1)}, s32[96,128]{1,0:T(8,128)}, u32[]{:S(2)}) copy-start(s32[96,128]{1,0:T(8,128)} %copy-done.19) | copy-start | bytes 147460
  136.9 9.9 %copy-start.22 = (s32[96,128]{1,0:T(8,128)S(1)}, s32[96,128]{1,0:T(8,128)}, u32[]{:S(2)}) copy-start(s32[96,128]{1,0:T(8,128)} %copy-done.21) | copy-start | bytes 147460
  142.4 44.7 %collective-permute-start.1 = (bf16[19,128,384]{2,1,0:T(8,128)(2,1)}, bf16[19,128,384]{2,1,0:T(8,128)(2,1)}, u32[]{:S(2)}, u32[]{:S(2)}) collective-permute-start(bf16[19,128,384]{2,1,0:T(8,128)(2,1)} %get-tuple-element.12), channel_id=1, source_target_pairs={{0,8},{4,12},{8,0},{12,4},{16,24},{20,28},{24,16},{28,20},{1,9},{5... | collective-permute-start | bytes 5603336 | tf_op jit(solution)/shard_map/ppermute | solution.py:93
  145.2 82.8 %collective-permute-start.2 = (bf16[19,128,384]{2,1,0:T(8,128)(2,1)}, bf16[19,128,384]{2,1,0:T(8,128)(2,1)}, u32[]{:S(2)}, u32[]{:S(2)}) collective-permute-start(bf16[19,128,384]{2,1,0:T(8,128)(2,1)} %get-tuple-element.14), channel_id=1, source_target_pairs={{0,16},{4,20},{8,24},{12,28},{16,0},{20,4},{24,8},{28,12},{1,17},{... | collective-permute-start | bytes 5603336 | tf_op jit(solution)/shard_map/ppermute | solution.py:93
  146.8 81.3 %collective-permute-start.3 = (bf16[19,128,384]{2,1,0:T(8,128)(2,1)}, bf16[19,128,384]{2,1,0:T(8,128)(2,1)}, u32[]{:S(2)}, u32[]{:S(2)}) collective-permute-start(bf16[19,128,384]{2,1,0:T(8,128)(2,1)} %get-tuple-element.13), channel_id=1, source_target_pairs={{0,24},{4,28},{8,16},{12,20},{16,8},{20,12},{24,0},{28,4},{1,25},{... | collective-permute-start | bytes 5603336 | tf_op jit(solution)/shard_map/ppermute | solution.py:93
  165.3 68.1 %copy-start.1 = (bf16[152,128,128]{2,1,0:T(8,128)(2,1)}, bf16[152,128,128]{2,1,0:T(8,128)(2,1)S(1)}, u32[]{:S(2)}) copy-start(bf16[152,128,128]{2,1,0:T(8,128)(2,1)S(1)} %copy.24) | copy-start | bytes 14942212
  233.4 43.7 %collective-permute-start.4 = (bf16[4,19,128,128]{3,2,1,0:T(8,128)(2,1)}, bf16[4,19,128,128]{3,2,1,0:T(8,128)(2,1)S(1)}, u32[]{:S(2)}, u32[]{:S(2)}) collective-permute-start(bf16[4,19,128,128]{3,2,1,0:T(8,128)(2,1)} %dynamic-slice_bitcast_fusion.1), channel_id=1, source_target_pairs={{0,4},{4,0},{8,12},{12,8},{16,20},{20,16},{24,28},{28,24},{1,5},{5... | collective-permute-start | bytes 7471112 | tf_op jit(solution)/shard_map/ppermute | solution.py:76
  272.0 49.1 %all-to-all-start = ((bf16[4,19,32,384]{3,2,1,0:T(8,128)(2,1)}), bf16[4,19,32,384]{3,2,1,0:T(8,128)(2,1)}, u32[]{:S(2)}, u32[]{:S(2)}) async-start(bf16[4,19,32,384]{3,2,1,0:T(8,128)(2,1)} %pad_maximum_fusion.2), calls=%async_computation | async-start | bytes 3735552 | tf_op jit(solution)/shard_map/all_to_all | solution.py:136
  277.1 8.4 %copy-start.3 = (bf16[19,32,2048]{2,1,0:T(8,128)(2,1)S(1)}, bf16[19,32,2048]{2,1,0:T(8,128)(2,1)}, u32[]{:S(2)}) copy-start(bf16[19,32,2048]{2,1,0:T(8,128)(2,1)} %param.13) | copy-start | bytes 7471108
  277.1 11.3 %copy-start.2 = (bf16[4,19,128,128]{3,2,1,0:T(8,128)(2,1)}, bf16[4,19,128,128]{3,2,1,0:T(8,128)(2,1)S(1)}, u32[]{:S(2)}) copy-start(bf16[4,19,128,128]{3,2,1,0:T(8,128)(2,1)S(1)} %collective-permute-done.4) | copy-start | bytes 7471108
  282.0 43.2 %collective-permute-start.5 = (bf16[19,128,128]{2,1,0:T(8,128)(2,1)}, bf16[19,128,128]{2,1,0:T(8,128)(2,1)S(1)}, u32[]{:S(2)}, u32[]{:S(2)}) collective-permute-start(bf16[19,128,128]{2,1,0:T(8,128)(2,1)} %get-tuple-element.15), channel_id=1, source_target_pairs={{0,8},{4,12},{8,0},{12,4},{16,24},{20,28},{24,16},{28,20},{1,9},{5... | collective-permute-start | bytes 1867784 | tf_op jit(solution)/shard_map/ppermute | solution.py:93
  283.3 42.0 %collective-permute-start.6 = (bf16[19,128,128]{2,1,0:T(8,128)(2,1)}, bf16[19,128,128]{2,1,0:T(8,128)(2,1)}, u32[]{:S(2)}, u32[]{:S(2)}) collective-permute-start(bf16[19,128,128]{2,1,0:T(8,128)(2,1)} %get-tuple-element.17), channel_id=1, source_target_pairs={{0,16},{4,20},{8,24},{12,28},{16,0},{20,4},{24,8},{28,12},{1,17},{... | collective-permute-start | bytes 1867784 | tf_op jit(solution)/shard_map/ppermute | solution.py:93
  284.1 41.2 %collective-permute-start.7 = (bf16[19,128,128]{2,1,0:T(8,128)(2,1)}, bf16[19,128,128]{2,1,0:T(8,128)(2,1)}, u32[]{:S(2)}, u32[]{:S(2)}) collective-permute-start(bf16[19,128,128]{2,1,0:T(8,128)(2,1)} %get-tuple-element.16), channel_id=1, source_target_pairs={{0,24},{4,28},{8,16},{12,20},{16,8},{20,12},{24,0},{28,4},{1,25},{... | collective-permute-start | bytes 1867784 | tf_op jit(solution)/shard_map/ppermute | solution.py:93
  328.4 19.8 %all-to-all-start.1 = ((bf16[4,19,32,128]{3,2,1,0:T(8,128)(2,1)}), bf16[4,19,32,128]{3,2,1,0:T(8,128)(2,1)S(1)}, u32[]{:S(2)}, u32[]{:S(2)}) async-start(bf16[4,19,32,128]{3,2,1,0:T(8,128)(2,1)} %pad_maximum_fusion.3), calls=%async_computation.1 | async-start | bytes 1245184 | tf_op jit(solution)/shard_map/all_to_all | solution.py:136
  348.2 4.4 %slice-start = ((s8[4980736]{0:T(1024)(128)(4,1)}), s8[4194304]{0:T(1024)(128)(4,1)S(1)}, s32[]{:S(2)}) async-start(s8[4980736]{0:T(1024)(128)(4,1)} %bitcast.122), calls=%async_computation.2 | async-start | bytes 8388608
  348.5 4.1 %slice-start.1 = ((s8[4980736]{0:T(1024)(128)(4,1)}), s8[786432]{0:T(1024)(128)(4,1)S(1)}, s32[]{:S(2)}) async-start(s8[4980736]{0:T(1024)(128)(4,1)} %bitcast.122), calls=%async_computation.3 | async-start | bytes 1572864
  354.0 4.7 %collective-permute-start.8 = (f32[19,1024]{1,0:T(8,128)S(1)}, f32[19,1024]{1,0:T(8,128)S(1)}, u32[]{:S(2)}, u32[]{:S(2)}) collective-permute-start(f32[19,1024]{1,0:T(8,128)S(1)} %fusion.27), channel_id=1, source_target_pairs={{0,1},{1,0},{2,3},{3,2},{4,5},{5,4},{6,7},{7,6},{8,9},{9,8},{10,11... | collective-permute-start | bytes 233480 | tf_op jit(solution)/shard_map/ppermute | solution.py:55
  358.7 6.1 %collective-permute-start.9 = (f32[19,1024]{1,0:T(8,128)S(1)}, f32[19,1024]{1,0:T(8,128)S(1)}, u32[]{:S(2)}, u32[]{:S(2)}) collective-permute-start(f32[19,1024]{1,0:T(8,128)S(1)} %add.327), channel_id=1, source_target_pairs={{0,2},{1,3},{2,0},{3,1},{4,6},{5,7},{6,4},{7,5},{8,10},{9,11},{10,... | collective-permute-start | bytes 233480 | tf_op jit(solution)/shard_map/ppermute | solution.py:55
